TPU v7x, 256 devices: a whole 4x4x8 slice. The times are simulated.
256 devices in a mesh: src: 8 (over z_hi, y), width: 32 (over z_lo, x, core).
Axes of the slice: x: 4, y: 4, z: 8 (z_hi: 2, z_lo: 4; z = z_hi * 4 + z_lo), core: 2. Of those that a mesh axis runs over, the one named last changes fastest.
Arguments:
- resid: bfloat16 [8, 512, 8192], P('src', None, 'width'), may hold values from -6 to 6
- enc_w: bfloat16 [8, 8192, 6144], P('src', 'width'), may hold values from -0.0625 to 0.0625
- enc_b: float32 [8, 6144], P('src'), may hold values from -3 to 3
- dec_w: bfloat16 [8, 6144, 8192], P('src', None, 'width'), may hold values from -0.078125 to 0.078125
- target: bfloat16 [512, 8192], P(None, 'width'), may hold values from -36 to 36
- norm_gain: float32 [8192], P('width'), may hold values from 0.5 to 1.5
- wq: bfloat16 [8192, 8192], P(None, 'width'), may hold values from -0.0625 to 0.0625
- wk: bfloat16 [8192, 1024], P('width'), may hold values from -0.0625 to 0.0625
- wv: bfloat16 [8192, 1024], P('width'), may hold values from -0.0625 to 0.0625
- prompt_ids: int32 [512], replicated, may hold values from 0 to 3, never falling along the last dimension, each value on 1 to 256 neighbouring positions
Outputs:
- mlp_out: bfloat16 [512, 8192], P('src', 'width')
- context: bfloat16 [512, 8192], P('src', 'width')
Inputs may be any that keep to these rules, and one draw needn't show every extreme that they name: `prompt_ids`: rows of one prompt are contiguous and numbered in increasing order; the longest prompt has 256 rows.
All inputs are finite; a program needn't handle non-finite values.
Results may differ from a plain program's by a relative error of at most 0.008.
Values may be sent and summed in bfloat16 or wider, within the bound.
No kernel may reach another device: no remote copies, remote signals or barrier semaphores. Data moves between devices by JAX's collectives and lax.ppermute only.
A program may use at most 128 MiB of HBM per device.

v0:
```python
import math

import jax
import jax.numpy as jnp
from jax import lax
from jax.sharding import PartitionSpec as P

HD = 128
GROUP = 8


def on_device(resid, enc_w, enc_b, dec_w, target, norm_gain, wq, wk, wv, prompt_ids):
    n_width = lax.axis_size("width")
    n_src = lax.axis_size("src")
    width_pos = lax.axis_index("width")
    rows_all = resid.shape[1]
    width_local = resid.shape[2]
    width_all = width_local * n_width
    feat_share = enc_w.shape[2] // n_width
    mlp = jnp.zeros((rows_all, width_local), jnp.float32)
    local_rows = resid[0]
    w_enc = enc_w[0]
    w_dec = dec_w[0]
    bias = enc_b[0]

    def encode_term(start, count, w_enc=w_enc, local_rows=local_rows):
        return lax.dot_general(
            w_enc, local_rows, (((0,), (1,)), ((), ())), preferred_element_type=jnp.float32
        )

    pre_share = lax.psum_scatter(
        encode_term(jnp.int32(0), feat_share * lax.axis_size("width")),
        "width",
        scatter_dimension=0,
        tiled=True,
    )
    my_bias = lax.dynamic_slice_in_dim(bias, width_pos * feat_share, feat_share, 0)
    feats_t = jnp.maximum(pre_share + my_bias[:, None], 0.0).astype(jnp.bfloat16)

    def decode_piece(total, piece, start, w_dec=w_dec):
        return lax.dot_general(
            piece, w_dec, (((0,), (0,)), ((), ())), preferred_element_type=jnp.float32
        )

    mlp = decode_piece(mlp, lax.all_gather(feats_t, "width", axis=0, tiled=True), jnp.int32(0))
    query_rows = rows_all // n_src
    row_start = lax.axis_index("src") * query_rows
    summed = lax.psum(mlp, "src")
    stream = target.astype(jnp.float32) + summed
    power = lax.psum(jnp.sum(stream * stream, axis=1), "width") / width_all
    normed = (stream * lax.rsqrt(power + 1e-05)[:, None] * norm_gain[None, :]).astype(jnp.bfloat16)
    full = lax.all_gather(normed, "width", axis=1, tiled=True)
    mlp_mine = lax.dynamic_slice_in_dim(summed, row_start, query_rows, 0)
    mlp_out = mlp_mine.astype(jnp.bfloat16)
    mine = lax.dynamic_slice_in_dim(full, row_start, query_rows, 0)
    query = jnp.dot(mine, wq, preferred_element_type=jnp.float32).astype(jnp.bfloat16)
    full_local = lax.dynamic_slice_in_dim(full, width_pos * width_local, width_local, 1)
    key_part = jnp.dot(full_local, wk, preferred_element_type=jnp.float32)
    value_part = jnp.dot(full_local, wv, preferred_element_type=jnp.float32)
    key_total, value_total = lax.psum((key_part, value_part), "width")
    keys_all = key_total.astype(jnp.bfloat16)
    values_all = value_total.astype(jnp.bfloat16)
    heads_here = wq.shape[1] // HD
    kv_index = width_pos * heads_here // GROUP
    key_head = lax.dynamic_slice_in_dim(keys_all, kv_index * HD, HD, 1)
    value_head = lax.dynamic_slice_in_dim(values_all, kv_index * HD, HD, 1)
    query3 = query.reshape(query_rows, heads_here, HD)
    scores = jnp.einsum(
        "qhd,sd->hqs", query3, key_head, preferred_element_type=jnp.float32
    ) / math.sqrt(HD)
    query_index = row_start + jnp.arange(query_rows, dtype=jnp.int32)
    key_index = jnp.arange(rows_all, dtype=jnp.int32)
    query_prompt = lax.dynamic_slice_in_dim(prompt_ids, row_start, query_rows, 0)
    allowed = (query_prompt[:, None] == prompt_ids[None, :]) & (
        key_index[None, :] <= query_index[:, None]
    )
    scores = jnp.where(allowed[None], scores, -1e30)
    peak = jnp.max(scores, axis=-1, keepdims=True)
    weights = jnp.exp(scores - peak)
    probs = (weights / jnp.sum(weights, axis=-1, keepdims=True)).astype(jnp.bfloat16)
    context = jnp.einsum("hqs,sd->qhd", probs, value_head, preferred_element_type=jnp.float32)
    return (mlp_out, context.reshape(query_rows, heads_here * HD).astype(jnp.bfloat16))


def solution(mesh):
    in_specs = (
        P("src", None, "width"),
        P("src", "width", None),
        P("src", None),
        P("src", None, "width"),
        P(None, "width"),
        P("width"),
        P(None, "width"),
        P("width", None),
        P("width", None),
        P(),
    )
    out_specs = (P("src", "width"), P("src", "width"))
    return jax.shard_map(
        on_device, mesh=mesh, in_specs=in_specs, out_specs=out_specs, check_vma=False
    )
```

profile of v0, /device:TPU:8, one launch (start us, length us, event | category | flops | bytes accessed | tf_op | source)
XLA Modules:
  0.0 693.4 jit_solution(18164416177999638944)
XLA Ops:
  7.2 0.0 copy-start
  7.2 0.0 reduce-scatter.2.cloned.1.call-start
  7.2 1.8 copy-done
  9.1 7.4 %fusion.3 = f32[6144,512]{1,0:T(8,128)} fusion(bf16[1,256,6144]{2,1,0:T(8,128)(2,1)S(1)} %copy-done, bf16[1,512,256]{2,1,0:T(8,128)(2,1)} %param.10), kind=kOutput, calls=%fused_computation.3 | convolution fusion | flops 1610612736 | bytes 15990784 | tf_op jit(solution)/shard_map/dot_general | solution.py:27
  16.4 0.0 reduce-scatter.2.cloned.1.call-update
  16.5 0.0 all-gather.3.cloned.1.call-start
  16.5 0.8 constant_dynamic-slice_fusion
  17.3 168.4 %reduce-scatter.2.cloned.1.call-done = f32[192,512]{1,0:T(8,128)} async-done(((f32[6144,512]{1,0:T(8,128)}), f32[192,512]{1,0:T(8,128)}) %reduce-scatter.2.cloned.1.call-update) | async-done | bytes 393232 | tf_op jit(solution)/shard_map/reduce_scatter | solution.py:31
  185.7 1.8 maximum_convert_fusion
  187.5 0.0 all-gather.3.cloned.1.call-update
  187.5 0.0 copy-start.1
  187.5 0.0 copy-start.3
  187.5 0.0 copy-start.2
  187.5 0.0 all-reduce.4.cloned.1.call-start
  187.6 61.3 %all-gather.3.cloned.1.call-done = bf16[6144,512]{1,0:T(8,128)(2,1)} async-done(((bf16[192,512]{1,0:T(8,128)(2,1)}), bf16[6144,512]{1,0:T(8,128)(2,1)}) %all-gather.3.cloned.1.call-update) | async-done | bytes 6291472 | tf_op jit(solution)/shard_map/all_gather | solution.py:45
  248.9 6.3 fusion.1
  255.2 0.0 all-reduce.4.cloned.1.call-update
  255.2 0.0 all-gather.5.cloned.1.call-start
  255.3 102.4 %all-reduce.4.cloned.1.call-done = f32[512,256]{1,0:T(8,128)} async-done(((f32[512,256]{1,0:T(8,128)}), f32[512,256]{1,0:T(8,128)}) %all-reduce.4.cloned.1.call-update) | async-done | bytes 524304 | tf_op jit(solution)/shard_map/psum | solution.py:48
  357.7 0.0 copy-done.1
  357.7 1.2 multiply_reduce_fusion
  358.9 67.4 %psum.29 = f32[512]{0:T(512)S(1)} all-reduce(f32[512]{0:T(512)S(1)} %multiply_reduce_fusion), channel_id=1, replica_groups=mesh['src'=8,'width'=32] {'width'}, use_global_device_ids=true, to_apply=%region_3.0 | all-reduce | flops 512 | bytes 4096 | tf_op jit(solution)/shard_map/psum | solution.py:50
  426.3 0.0 copy-done.3
  426.3 1.9 multiply_convert_fusion
  428.2 0.0 all-gather.5.cloned.1.call-update
  428.3 0.0 copy-done.2
  428.3 0.1 dynamic_slice.25
  428.4 0.1 fusion.21
  428.5 1.5 dynamic-slice_convert_fusion.2
  429.9 83.2 %all-gather.5.cloned.1.call-done = bf16[512,8192]{1,0:T(8,128)(2,1)} async-done(((bf16[512,256]{1,0:T(8,128)(2,1)}), bf16[512,8192]{1,0:T(8,128)(2,1)}) %all-gather.5.cloned.1.call-update) | async-done | bytes 8388624 | tf_op jit(solution)/shard_map/all_gather | solution.py:52
  513.1 3.0 fusion.15
  516.1 2.9 fusion.13
  518.9 161.6 %all-reduce.5 = (bf16[512,1024]{1,0:T(8,128)(2,1)}, bf16[512,1024]{1,0:T(8,128)(2,1)}) all-reduce(f32[512,1024]{1,0:T(8,128)} %fusion.15, f32[512,1024]{1,0:T(8,128)} %fusion.13), channel_id=1, replica_groups=mesh['src'=8,'width'=32] {'width'}, use_global_device_ids=true, to_apply=%region_4.0 | all-reduce | flops 1048576 | bytes 6291456 | tf_op jit(solution)/shard_map/psum | solution.py:60
  680.5 3.3 fusion.9
  683.8 1.3 fusion.42
  685.1 1.1 fusion.10
  686.2 0.6 copy.28
  (2 shorter events, 0.0 us)
Async XLA Ops:
  7.2 1.9 copy-start
  7.2 178.5 %reduce-scatter.2.cloned.1.call-start = ((), (), s32[]{:S(2)}) async-start(), calls=%async_computation.1 | async-start | bytes 12976128 | tf_op jit(solution)/shard_map/reduce_scatter | solution.py:31
  16.5 232.4 %all-gather.3.cloned.1.call-start = ((), (), s32[]{:S(2)}) async-start(), calls=%async_computation.2 | async-start | bytes 6488064 | tf_op jit(solution)/shard_map/all_gather | solution.py:45
  187.5 170.2 %copy-start.1 = (bf16[512,256]{1,0:T(8,128)(2,1)S(1)}, bf16[512,256]{1,0:T(8,128)(2,1)}, u32[]{:S(2)}) copy-start(bf16[512,256]{1,0:T(8,128)(2,1)} %param.14) | copy-start | bytes 786436
  187.5 238.8 %copy-start.3 = (f32[256]{0:T(256)S(1)}, f32[256]{0:T(256)}, u32[]{:S(2)}) copy-start(f32[256]{0:T(256)} %param.15) | copy-start | bytes 3076
  187.5 240.8 %copy-start.2 = (s32[512]{0:T(512)S(1)}, s32[512]{0:T(512)}, u32[]{:S(2)}) copy-start(s32[512]{0:T(512)} %param.19) | copy-start | bytes 6148
  187.5 170.2 %all-reduce.4.cloned.1.call-start = ((), (), s32[]{:S(2)}) async-start(), calls=%async_computation.3 | async-start | bytes 1048576 | tf_op jit(solution)/shard_map/psum | solution.py:48
  255.2 257.9 %all-gather.5.cloned.1.call-start = ((), (), s32[]{:S(2)}) async-start(), calls=%async_computation.4 | async-start | bytes 8650752 | tf_op jit(solution)/shard_map/all_gather | solution.py:52
Sparse Core Ops, SparseCore 0:
  16.6 169.0 reduce-scatter.1
  187.6 61.2 all-gather.2
  255.4 102.3 all-reduce.3
  428.4 84.6 all-gather.4
where the time goes:
time: 694 us; the launch traced here: 693 us
  waiting for transfers between devices  415 us (60%)
  blocking collectives  229 us (33%)
  matrix products  25.3 us (4%)
  between operations  13.9 us (2%)
    reduce_scatter x1, waiting for transfers between devices, on_device(): lax.psum_scatter(encode_term(jnp.int32(0), feat_share * lax.axis_size('wi...  168 us
    psum x1, blocking collectives, on_device(): key_total, value_total = lax.psum((key_part, value_part), 'width')  162 us
    psum x1, waiting for transfers between devices, on_device(): summed = lax.psum(mlp, 'src')  102 us
    all_gather x1, waiting for transfers between devices, on_device(): full = lax.all_gather(normed, 'width', axis=1, tiled=True)  83.2 us
    psum x1, blocking collectives, on_device(): power = lax.psum(jnp.sum(stream * stream, axis=1), 'width') / width_all  67.4 us
    all_gather x1, waiting for transfers between devices, on_device(): lax.all_gather(feats_t, 'width', axis=0, tiled=True)  61.3 us
  transfers between devices with their start and end apart: 4, of which 4 were waited for; matrix products, arithmetic and copies ran while one was open for 0% of the time, Pallas kernels for 0%

commit v1 on v0

v1 whole, which is shorter than its diff:
```python
import math

import jax
import jax.numpy as jnp
from jax import lax
from jax.sharding import Mesh
from jax.sharding import PartitionSpec as P

HD = 128
GROUP = 8
WIDTH = ("wc", "core")
SWAP = [(0, 1), (1, 0)]


def contract0(a, b):
    return lax.dot_general(a, b, (((0,), (0,)), ((), ())), preferred_element_type=jnp.float32)


def on_device(resid, enc_w, enc_b, dec_w, target, norm_gain, wq, wk, wv, prompt_ids):
    n_wc = lax.axis_size("wc")
    n_core = lax.axis_size("core")
    n_src = lax.axis_size("src")
    core = lax.axis_index("core")
    chip = lax.axis_index("wc")
    src = lax.axis_index("src")
    width_pos = chip * n_core + core
    rows_all = resid.shape[1]
    width_local = resid.shape[2]
    width_all = width_local * n_wc * n_core
    feats_all = enc_w.shape[2]
    half = feats_all // 2
    share = half // n_wc
    other = 1 - core

    x = resid[0]
    we = enc_w[0]
    we_mine = lax.dynamic_slice_in_dim(we, core * half, half, 1)
    we_give = lax.dynamic_slice_in_dim(we, other * half, half, 1)
    we_got = lax.ppermute(we_give, "core", SWAP)
    x_got = lax.ppermute(x, "core", SWAP)
    pre = lax.dot_general(we_mine, x, (((0,), (1,)), ((), ())), preferred_element_type=jnp.float32)
    pre = pre + lax.dot_general(we_got, x_got, (((0,), (1,)), ((), ())), preferred_element_type=jnp.float32)
    pre_share = lax.psum_scatter(pre, "wc", scatter_dimension=0, tiled=True)
    bias = lax.dynamic_slice_in_dim(enc_b[0], core * half + chip * share, share, 0)
    feats_t = jnp.maximum(pre_share + bias[:, None], 0.0).astype(jnp.bfloat16)
    feats_half = lax.all_gather(feats_t, "wc", axis=0, tiled=True)

    wd = dec_w[0]
    wd_mine = lax.dynamic_slice_in_dim(wd, core * half, half, 0)
    wd_give = lax.dynamic_slice_in_dim(wd, other * half, half, 0)
    wd_got = lax.ppermute(wd_give, "core", SWAP)
    part_mine = contract0(feats_half, wd_mine)
    part_other = contract0(feats_half, wd_got)
    mlp_layer = part_mine + lax.ppermute(part_other, "core", SWAP)

    query_rows = rows_all // n_src
    row_start = src * query_rows
    mlp = lax.psum_scatter(mlp_layer, "src", scatter_dimension=0, tiled=True)
    mlp_out = mlp.astype(jnp.bfloat16)
    tgt = lax.dynamic_slice_in_dim(target, row_start, query_rows, 0)
    stream = tgt.astype(jnp.float32) + mlp
    stream_full = lax.all_gather(stream, WIDTH, axis=1, tiled=True)
    gain_full = lax.all_gather(norm_gain, WIDTH, axis=0, tiled=True)
    power = jnp.sum(stream_full * stream_full, axis=1) / width_all
    scale = lax.rsqrt(power + 1e-05)[:, None]
    normed_full = (stream_full * scale * gain_full[None, :]).astype(jnp.bfloat16)
    normed_loc = (stream * scale * norm_gain[None, :]).astype(jnp.bfloat16)

    query = jnp.dot(normed_full, wq, preferred_element_type=jnp.float32).astype(jnp.bfloat16)
    key_part = jnp.dot(normed_loc, wk, preferred_element_type=jnp.float32)
    value_part = jnp.dot(normed_loc, wv, preferred_element_type=jnp.float32)
    key_total, value_total = lax.psum((key_part, value_part), WIDTH)
    heads_here = wq.shape[1] // HD
    kv_index = width_pos * heads_here // GROUP
    key_head = lax.dynamic_slice_in_dim(key_total, kv_index * HD, HD, 1).astype(jnp.bfloat16)
    value_head = lax.dynamic_slice_in_dim(value_total, kv_index * HD, HD, 1).astype(jnp.bfloat16)
    key_head = lax.all_gather(key_head, "src", axis=0, tiled=True)
    value_head = lax.all_gather(value_head, "src", axis=0, tiled=True)

    query3 = query.reshape(query_rows, heads_here, HD)
    scores = jnp.einsum(
        "qhd,sd->hqs", query3, key_head, preferred_element_type=jnp.float32
    ) / math.sqrt(HD)
    query_index = row_start + jnp.arange(query_rows, dtype=jnp.int32)
    key_index = jnp.arange(rows_all, dtype=jnp.int32)
    query_prompt = lax.dynamic_slice_in_dim(prompt_ids, row_start, query_rows, 0)
    allowed = (query_prompt[:, None] == prompt_ids[None, :]) & (
        key_index[None, :] <= query_index[:, None]
    )
    scores = jnp.where(allowed[None], scores, -1e30)
    peak = jnp.max(scores, axis=-1, keepdims=True)
    weights = jnp.exp(scores - peak)
    probs = (weights / jnp.sum(weights, axis=-1, keepdims=True)).astype(jnp.bfloat16)
    context = jnp.einsum("hqs,sd->qhd", probs, value_head, preferred_element_type=jnp.float32)
    return (mlp_out, context.reshape(query_rows, heads_here * HD).astype(jnp.bfloat16))


def solution(mesh):
    n_src = mesh.shape["src"]
    n_width = mesh.shape["width"]
    fine = Mesh(mesh.devices.reshape(n_src, n_width // 2, 2), ("src", "wc", "core"))
    in_specs = (
        P("src", None, WIDTH),
        P("src", WIDTH, None),
        P("src", None),
        P("src", None, WIDTH),
        P(None, WIDTH),
        P(WIDTH),
        P(None, WIDTH),
        P(WIDTH, None),
        P(WIDTH, None),
        P(),
    )
    out_specs = (P("src", WIDTH), P("src", WIDTH))
    return jax.shard_map(
        on_device, mesh=fine, in_specs=in_specs, out_specs=out_specs, check_vma=False
    )
```

time: 694 us -> 603 us (0.87)
  waiting for transfers between devices: 415 us -> 285 us
  blocking collectives: 229 us -> 268 us
    all_gather x0 -> x3, blocking collectives: none -> 127 us  [the longest x1 43.8 us: on_device(): value_head = lax.all_gather(value_head, 'src', axis=0, tiled=True)]
    psum x1 -> x0, waiting for transfers between devices: 102 us -> none  [on_device(): summed = lax.psum(mlp, 'src')]
    psum x2 -> x1, blocking collectives: 229 us -> 141 us  [on_device(): key_total, value_total = lax.psum((key_part, value_part), WIDTH)]
    all_gather x2, waiting for transfers between devices: 144 us -> 92.3 us  [the longest x1 76.9 us: on_device(): feats_half = lax.all_gather(feats_t, 'wc', axis=0, tiled=True)]
    reduce_scatter x1 -> x2, waiting for transfers between devices: 168 us -> 186 us  [the longest x1 103 us: on_device(): pre_share = lax.psum_scatter(pre, 'wc', scatter_dimension=0, tiled=True)]
    dot_general x5 -> x7, matrix products: 22.8 us -> 18.2 us  [the longest x2 5.94 us: contract0(): lax.dot_general(a, b, (((0,), (0,)), ((), ())), preferred_element_type=jn...]
  transfers between devices with their start and end apart: 4 -> 8, of which waited for: 4 -> 6; matrix products, arithmetic and copies ran while one was open for 0% -> 1% of each run, Pallas kernels for 0% -> 0%
where the time goes in v1:
time: 603 us; the launch traced here: 602 us
  waiting for transfers between devices  285 us (47%)
  blocking collectives  268 us (44%)
  matrix products  20.3 us (3%)
  between operations  14 us (2%)
  local copies, waits for them, and re-layouts  7.55 us (1%)
  other arithmetic  6.22 us (1%)
    psum x1, blocking collectives, on_device(): key_total, value_total = lax.psum((key_part, value_part), WIDTH)  141 us
    reduce_scatter x1, waiting for transfers between devices, on_device(): pre_share = lax.psum_scatter(pre, 'wc', scatter_dimension=0, tiled=True)  103 us
    reduce_scatter x1, waiting for transfers between devices, on_device(): mlp = lax.psum_scatter(mlp_layer, 'src', scatter_dimension=0, tiled=True)  83.6 us
    all_gather x1, waiting for transfers between devices, on_device(): feats_half = lax.all_gather(feats_t, 'wc', axis=0, tiled=True)  76.9 us
    all_gather x1, blocking collectives, on_device(): value_head = lax.all_gather(value_head, 'src', axis=0, tiled=True)  43.8 us
    all_gather x1, blocking collectives, on_device(): key_head = lax.all_gather(key_head, 'src', axis=0, tiled=True)  42.8 us
    all_gather x1, blocking collectives, on_device(): gain_full = lax.all_gather(norm_gain, WIDTH, axis=0, tiled=True)  40.3 us
    all_gather x1, waiting for transfers between devices, on_device(): stream_full = lax.all_gather(stream, WIDTH, axis=1, tiled=True)  15.4 us
  transfers between devices with their start and end apart: 8, of which 6 were waited for; matrix products, arithmetic and copies ran while one was open for 1% of the time, Pallas kernels for 0%

profile of v1, /device:TPU:8, one launch (start us, length us, event | category | flops | bytes accessed | tf_op | source)
XLA Modules:
  0.0 601.5 jit_solution(9003281034998828032)
XLA Ops:
  7.2 0.0 copy-start
  7.2 0.0 reduce-scatter.3.cloned.1.call-start
  7.2 1.8 copy-done
  9.1 1.3 dynamic-slice_bitcast_fusion.1
  10.3 0.0 collective-permute-start
  10.4 0.5 collective-permute-start.1
  10.9 1.0 fusion.3
  11.9 2.6 collective-permute-done.1
  14.5 0.0 collective-permute-done
  14.5 5.2 convolution_add_fusion
  19.7 0.0 reduce-scatter.3.cloned.1.call-update
  19.7 0.0 all-gather.4.cloned.1.call-start
  19.8 0.8 constant_dynamic-slice_fusion
  20.5 102.7 %reduce-scatter.3.cloned.1.call-done = f32[192,512]{1,0:T(8,128)} async-done(((f32[3072,512]{1,0:T(8,128)}), f32[192,512]{1,0:T(8,128)}) %reduce-scatter.3.cloned.1.call-update) | async-done | bytes 393232 | tf_op jit(solution)/shard_map/reduce_scatter | solution.py:43
  123.2 1.8 maximum_convert_fusion
  125.0 0.0 all-gather.4.cloned.1.call-update
  125.0 0.0 reduce-scatter.5.cloned.1.call-start
  125.1 1.5 dynamic-slice_bitcast_fusion
  126.6 0.1 collective-permute-start.2
  126.7 3.5 collective-permute-done.2
  130.2 76.9 %all-gather.4.cloned.1.call-done = bf16[3072,512]{1,0:T(8,128)(2,1)} async-done(((bf16[192,512]{1,0:T(8,128)(2,1)}), bf16[3072,512]{1,0:T(8,128)(2,1)}) %all-gather.4.cloned.1.call-update) | async-done | bytes 3145744 | tf_op jit(solution)/shard_map/all_gather | solution.py:46
  207.2 3.5 fusion.41
  210.7 0.0 copy-start.6
  210.7 0.0 copy-start.5
  210.7 0.1 collective-permute-start.3
  210.8 2.4 fusion.1
  213.3 0.9 add.81
  214.1 0.0 reduce-scatter.5.cloned.1.call-update
  214.2 0.0 all-gather.6.cloned.1.call-start
  214.2 83.6 %reduce-scatter.5.cloned.1.call-done = f32[64,256]{1,0:T(8,128)} async-done(((f32[512,256]{1,0:T(8,128)}), f32[64,256]{1,0:T(8,128)}) %reduce-scatter.5.cloned.1.call-update) | async-done | bytes 65552 | tf_op jit(solution)/shard_map/reduce_scatter | solution.py:58
  297.8 1.6 convert_add_fusion
  299.4 0.0 all-gather.6.cloned.1.call-update
  299.5 0.1 dynamic_slice.46
  299.5 40.3 %all-gather = f32[32,1,256]{2,1,0:T(1,128)S(1)} all-gather(f32[1,1,256]{2,1,0:T(1,128)S(1)} %bitcast.66), channel_id=1, replica_groups=mesh['src'=8,'wc'=16,'core'=2] {'wc','core'}, dimensions={0}, use_global_device_ids=true | all-gather | bytes 33792 | tf_op jit(solution)/shard_map/all_gather | solution.py:63
  339.9 0.1 fusion.17
  340.0 15.4 %all-gather.6.cloned.1.call-done = f32[64,8192]{1,0:T(8,128)} async-done(((f32[64,256]{1,0:T(8,128)}), f32[64,8192]{1,0:T(8,128)}) %all-gather.6.cloned.1.call-update) | async-done | bytes 2097168 | tf_op jit(solution)/shard_map/all_gather | solution.py:62
  355.4 1.9 multiply_reduce_fusion
  357.3 1.3 fusion.34
  358.6 1.0 fusion.35
  359.6 140.9 %all-reduce.2 = (bf16[64,1024]{1,0:T(8,128)(2,1)}, bf16[64,1024]{1,0:T(8,128)(2,1)}) all-reduce(f32[64,1024]{1,0:T(8,128)} %fusion.35, f32[64,1024]{1,0:T(8,128)S(1)} %fusion.34), channel_id=1, replica_groups=mesh['src'=8,'wc'=16,'core'=2] {'wc','core'}, use_global_device_ids=true, to_apply=%region_3.0 | all-reduce | flops 131072 | bytes 786432 | tf_op jit(solution)/shard_map/psum | solution.py:72
  500.5 0.7 dynamic-slice_convert_fusion
  501.2 42.8 %all_gather.18 = bf16[512,128]{1,0:T(8,128)(2,1)S(1)} all-gather(bf16[64,128]{1,0:T(8,128)(2,1)S(1)} %dynamic-slice_convert_fusion), channel_id=1, replica_groups=mesh['src'=8,'wc'=16,'core'=2] {'src'}, dimensions={0}, use_global_device_ids=true | all-gather | bytes 147456 | tf_op jit(solution)/shard_map/all_gather | solution.py:77
  544.0 0.7 dynamic-slice_convert_fusion.1
  544.7 43.8 %all_gather.17 = bf16[512,128]{1,0:T(8,128)(2,1)S(1)} all-gather(bf16[64,128]{1,0:T(8,128)(2,1)S(1)} %dynamic-slice_convert_fusion.1), channel_id=1, replica_groups=mesh['src'=8,'wc'=16,'core'=2] {'src'}, dimensions={0}, use_global_device_ids=true | all-gather | bytes 147456 | tf_op jit(solution)/shard_map/all_gather | solution.py:78
  588.5 3.7 fusion.11
  592.2 1.0 fusion.36
  593.2 1.2 fusion.12
  594.3 0.6 copy.30
  (13 shorter events, 0.0 us)
Async XLA Ops:
  7.2 1.9 copy-start
  7.2 3.2 copy-start.4
  7.2 116.0 %reduce-scatter.3.cloned.1.call-start = ((), (), s32[]{:S(2)}) async-start(), calls=%async_computation.2 | async-start | bytes 6684672 | tf_op jit(solution)/shard_map/reduce_scatter | solution.py:43
  10.3 4.1 collective-permute-start
  10.4 4.1 collective-permute-start.1
  19.7 187.5 %all-gather.4.cloned.1.call-start = ((), (), s32[]{:S(2)}) async-start(), calls=%async_computation.3 | async-start | bytes 3342336 | tf_op jit(solution)/shard_map/all_gather | solution.py:46
  125.0 172.8 %reduce-scatter.5.cloned.1.call-start = ((), (), s32[]{:S(2)}) async-start(), calls=%async_computation.4 | async-start | bytes 589824 | tf_op jit(solution)/shard_map/reduce_scatter | solution.py:58
  126.6 3.6 collective-permute-start.2
  207.2 3.7 copy-start.1
  210.7 88.8 %copy-start.6 = (s32[512]{0:T(512)S(1)}, s32[512]{0:T(512)}, u32[]{:S(2)}) copy-start(s32[512]{0:T(512)} %param.19) | copy-start | bytes 6148
  210.7 88.8 %copy-start.5 = (f32[256]{0:T(256)S(1)}, f32[256]{0:T(256)}, u32[]{:S(2)}) copy-start(f32[256]{0:T(256)} %param.15) | copy-start | bytes 3076
  210.7 2.5 collective-permute-start.3
  214.2 141.2 %all-gather.6.cloned.1.call-start = ((), (), s32[]{:S(2)}) async-start(), calls=%async_computation.5 | async-start | bytes 2162688 | tf_op jit(solution)/shard_map/all_gather | solution.py:62
  299.4 59.2 %copy-start.2 = (f32[64,256]{1,0:T(8,128)S(1)}, f32[64,256]{1,0:T(8,128)}, u32[]{:S(2)}) copy-start(f32[64,256]{1,0:T(8,128)} %get-tuple-element.4) | copy-start | bytes 196612
  355.3 3.3 copy-start.3
Sparse Core Ops, SparseCore 0:
  19.8 103.3 reduce-scatter.2
  125.2 81.9 all-gather.3
  214.3 83.5 reduce-scatter.4
  299.6 55.7 all-gather.5

commit v2 on v1

v2 whole, which is shorter than its diff:
```python
import math

import jax
import jax.numpy as jnp
from jax import lax
from jax.sharding import Mesh
from jax.sharding import PartitionSpec as P

HD = 128
GROUP = 8
WIDTH = ("wch", "wcl", "core")
CHIP = ("wch", "wcl")
SWAP = [(0, 1), (1, 0)]


def contract0(a, b):
    return lax.dot_general(a, b, (((0,), (0,)), ((), ())), preferred_element_type=jnp.float32)


def on_device(resid, enc_w, enc_b, dec_w, target, norm_gain, wq, wk, wv, prompt_ids):
    n_chip = lax.axis_size(CHIP)
    n_core = lax.axis_size("core")
    n_src = lax.axis_size("src")
    core = lax.axis_index("core")
    chip = lax.axis_index(CHIP)
    src = lax.axis_index("src")
    width_pos = chip * n_core + core
    rows_all = resid.shape[1]
    width_local = resid.shape[2]
    width_all = width_local * n_chip * n_core
    feats_all = enc_w.shape[2]
    share = feats_all // (n_chip * n_core)
    other = 1 - core

    x = resid[0]
    we = enc_w[0].reshape(width_local, n_chip, n_core, share)
    we_mine = lax.dynamic_index_in_dim(we, core, 2, keepdims=False).reshape(width_local, n_chip * share)
    we_give = lax.dynamic_index_in_dim(we, other, 2, keepdims=False).reshape(width_local, n_chip * share)
    we_got = lax.ppermute(we_give, "core", SWAP)
    x_got = lax.ppermute(x, "core", SWAP)
    pre = lax.dot_general(we_mine, x, (((0,), (1,)), ((), ())), preferred_element_type=jnp.float32)
    pre = pre + lax.dot_general(we_got, x_got, (((0,), (1,)), ((), ())), preferred_element_type=jnp.float32)
    pre_share = lax.psum_scatter(pre, CHIP, scatter_dimension=0, tiled=True)
    bias = lax.dynamic_slice_in_dim(enc_b[0], width_pos * share, share, 0)
    feats_t = jnp.maximum(pre_share + bias[:, None], 0.0).astype(jnp.bfloat16)
    feats = lax.all_gather(feats_t, WIDTH, axis=0, tiled=True)
    mlp_layer = contract0(feats, dec_w[0])

    query_rows = rows_all // n_src
    row_start = src * query_rows
    mlp = lax.psum_scatter(mlp_layer, "src", scatter_dimension=0, tiled=True)
    mlp_out = mlp.astype(jnp.bfloat16)
    tgt = lax.dynamic_slice_in_dim(target, row_start, query_rows, 0)
    stream = tgt.astype(jnp.float32) + mlp
    packed = jnp.concatenate([stream, norm_gain[None, :]], axis=0)
    packed_full = lax.all_gather(packed, WIDTH, axis=1, tiled=True)
    stream_full = packed_full[:query_rows]
    gain_full = packed_full[query_rows]
    power = jnp.sum(stream_full * stream_full, axis=1) / width_all
    scale = lax.rsqrt(power + 1e-05)[:, None]
    normed_full = (stream_full * scale * gain_full[None, :]).astype(jnp.bfloat16)
    normed_loc = (stream * scale * norm_gain[None, :]).astype(jnp.bfloat16)

    query = jnp.dot(normed_full, wq, preferred_element_type=jnp.float32).astype(jnp.bfloat16)
    n_kv = wk.shape[1] // HD
    key_part = jnp.dot(normed_loc, wk, preferred_element_type=jnp.float32).reshape(query_rows, n_kv, 1, HD)
    value_part = jnp.dot(normed_loc, wv, preferred_element_type=jnp.float32).reshape(query_rows, n_kv, 1, HD)
    kv_part = jnp.concatenate([key_part, value_part], axis=2).reshape(query_rows, n_kv * 2 * HD)
    kv_share = lax.psum_scatter(kv_part, WIDTH, scatter_dimension=1, tiled=True).astype(jnp.bfloat16)
    kv_all = lax.all_gather(kv_share, ("src", "wcl", "core"), axis=0, tiled=False)
    quarter = kv_share.shape[1]
    kv_all = kv_all.reshape(n_src, -1, query_rows, quarter).transpose(0, 2, 1, 3).reshape(rows_all, -1)
    key_head = kv_all[:, :HD]
    value_head = kv_all[:, HD:]
    heads_here = wq.shape[1] // HD

    query3 = query.reshape(query_rows, heads_here, HD)
    scores = jnp.einsum(
        "qhd,sd->hqs", query3, key_head, preferred_element_type=jnp.float32
    ) / math.sqrt(HD)
    query_index = row_start + jnp.arange(query_rows, dtype=jnp.int32)
    key_index = jnp.arange(rows_all, dtype=jnp.int32)
    query_prompt = lax.dynamic_slice_in_dim(prompt_ids, row_start, query_rows, 0)
    allowed = (query_prompt[:, None] == prompt_ids[None, :]) & (
        key_index[None, :] <= query_index[:, None]
    )
    scores = jnp.where(allowed[None], scores, -1e30)
    peak = jnp.max(scores, axis=-1, keepdims=True)
    weights = jnp.exp(scores - peak)
    probs = (weights / jnp.sum(weights, axis=-1, keepdims=True)).astype(jnp.bfloat16)
    context = jnp.einsum("hqs,sd->qhd", probs, value_head, preferred_element_type=jnp.float32)
    return (mlp_out, context.reshape(query_rows, heads_here * HD).astype(jnp.bfloat16))


def solution(mesh):
    n_src = mesh.shape["src"]
    n_width = mesh.shape["width"]
    fine = Mesh(mesh.devices.reshape(n_src, n_width // 4, 2, 2), ("src", "wch", "wcl", "core"))
    in_specs = (
        P("src", None, WIDTH),
        P("src", WIDTH, None),
        P("src", None),
        P("src", None, WIDTH),
        P(None, WIDTH),
        P(WIDTH),
        P(None, WIDTH),
        P(WIDTH, None),
        P(WIDTH, None),
        P(),
    )
    out_specs = (P("src", WIDTH), P("src", WIDTH))
    return jax.shard_map(
        on_device, mesh=fine, in_specs=in_specs, out_specs=out_specs, check_vma=False
    )
```

time: 603 us -> 556 us (0.922); the launches traced: 602 us -> 548 us
  blocking collectives: 268 us -> 45.1 us
  waiting for transfers between devices: 285 us -> 450 us
  local copies, waits for them, and re-layouts: 7.55 us -> 14.5 us
    unnamed x4 -> x6, waiting for transfers between devices: 0.07 us -> 142 us
    psum x1 -> x0, blocking collectives: 141 us -> none  [on_device(): key_total, value_total = lax.psum((key_part, value_part), WIDTH)]
    all_gather x3 -> x1, blocking collectives: 127 us -> 45.1 us  [on_device(): lax.all_gather(kv_share, ('src', 'wcl', 'core'), axis=0, tiled=False)]
    all_gather x2, waiting for transfers between devices: 92.3 us -> 118 us  [the longest x1 61.6 us: on_device(): feats = lax.all_gather(feats_t, WIDTH, axis=0, tiled=True)]
    unnamed x14 -> x17, local copies, waits for them, and re-layouts: 1.85 us -> 8.13 us
  transfers between devices with their start and end apart: 8 -> 7, of which waited for: 6 -> 6; matrix products, arithmetic and copies ran while one was open for 1% -> 1% of each run, Pallas kernels for 0% -> 0%
where the time goes in v2:
time: 556 us; the launch traced here: 548 us
  waiting for transfers between devices  450 us (81%)
  blocking collectives  45.1 us (8%)
  matrix products  16.4 us (3%)
  local copies, waits for them, and re-layouts  14.5 us (3%)
  between operations  14 us (3%)
  other arithmetic  7.24 us (1%)
    unnamed x6, waiting for transfers between devices  142 us
    reduce_scatter x1, waiting for transfers between devices, on_device(): pre_share = lax.psum_scatter(pre, CHIP, scatter_dimension=0, tiled=True)  103 us
    reduce_scatter x1, waiting for transfers between devices, on_device(): mlp = lax.psum_scatter(mlp_layer, 'src', scatter_dimension=0, tiled=True)  84.3 us
    all_gather x1, waiting for transfers between devices, on_device(): feats = lax.all_gather(feats_t, WIDTH, axis=0, tiled=True)  61.6 us
    all_gather x1, waiting for transfers between devices, on_device(): packed_full = lax.all_gather(packed, WIDTH, axis=1, tiled=True)  56.1 us
    all_gather x1, blocking collectives, on_device(): lax.all_gather(kv_share, ('src', 'wcl', 'core'), axis=0, tiled=False)  45.1 us
  transfers between devices with their start and end apart: 7, of which 6 were waited for; matrix products, arithmetic and copies ran while one was open for 1% of the time, Pallas kernels for 0%

profile of v2, /device:TPU:8, one launch (start us, length us, event | category | flops | bytes accessed | tf_op | source)
XLA Modules:
  0.0 547.6 jit_solution(193489889811230243)
XLA Ops:
  7.2 0.0 copy-start
  7.2 0.0 reduce-scatter.6.cloned.1.call-start
  7.2 4.8 copy.20
  12.0 2.2 constant_dynamic-slice_fusion.1
  14.3 0.1 collective-permute-start
  14.4 0.5 collective-permute-start.1
  14.9 1.0 fusion.16
  15.9 2.3 collective-permute-done.1
  18.1 0.0 collective-permute-done
  18.2 3.6 convolution_add_fusion
  21.8 0.0 reduce-scatter.6.cloned.1.call-update
  21.8 0.0 all-gather.4.cloned.1.call-start
  21.9 0.8 constant_dynamic-slice_fusion
  22.6 103.5 %reduce-scatter.6.cloned.1.call-done = f32[192,512]{1,0:T(8,128)} async-done(((f32[3072,512]{1,0:T(8,128)}), f32[192,512]{1,0:T(8,128)}) %reduce-scatter.6.cloned.1.call-update) | async-done | bytes 393232 | tf_op jit(solution)/shard_map/reduce_scatter | solution.py:43
  126.1 1.8 maximum_convert_fusion
  127.9 0.0 all-gather.4.cloned.1.call-update
  127.9 0.0 copy-start.4
  127.9 0.0 reduce-scatter.8.cloned.1.call-start
  127.9 61.6 %all-gather.4.cloned.1.call-done = bf16[6144,512]{1,0:T(8,128)(2,1)} async-done(((bf16[192,512]{1,0:T(8,128)(2,1)}), bf16[6144,512]{1,0:T(8,128)(2,1)}) %all-gather.4.cloned.1.call-update) | async-done | bytes 6291472 | tf_op jit(solution)/shard_map/all_gather | solution.py:46
  189.6 0.0 copy-done
  189.6 5.4 fusion.1
  195.0 0.0 reduce-scatter.8.cloned.1.call-update
  195.0 0.0 all-gather.6.cloned.1.call-start
  195.1 84.3 %reduce-scatter.8.cloned.1.call-done = f32[64,256]{1,0:T(8,128)} async-done(((f32[512,256]{1,0:T(8,128)}), f32[64,256]{1,0:T(8,128)}) %reduce-scatter.8.cloned.1.call-update) | async-done | bytes 65552 | tf_op jit(solution)/shard_map/reduce_scatter | solution.py:51
  279.3 1.5 convert_add_fusion
  280.9 0.6 pad_maximum_fusion.1
  281.5 0.0 all-gather.6.cloned.1.call-update
  281.5 0.0 reduce-scatter.10.cloned.1.call-start
  281.6 56.1 %all-gather.6.cloned.1.call-done = f32[65,8192]{1,0:T(8,128)} async-done(((f32[65,256]{1,0:T(8,128)}), f32[65,8192]{1,0:T(8,128)}) %all-gather.6.cloned.1.call-update) | async-done | bytes 2129936 | tf_op jit(solution)/shard_map/all_gather | solution.py:56
  337.7 1.9 multiply_reduce_fusion
  339.6 0.2 convolution_bitcast_fusion.1
  339.9 0.0 copy-start.5
  339.9 0.2 convolution_bitcast_fusion
  340.2 0.0 slice-start
  340.3 1.3 pad_maximum_fusion
  341.5 2.4 copy.31
  343.9 0.0 reduce-scatter.10.cloned.1.call-update
  343.9 0.1 dynamic_slice.20
  344.0 0.1 fusion.11
  344.1 3.7 fusion.7
  347.8 141.9 %reduce-scatter.10.cloned.1.call-done = f32[64,64]{1,0:T(8,128)} async-done(((f32[2048,64]{1,0:T(8,128)}), f32[64,64]{1,0:T(8,128)}) %reduce-scatter.10.cloned.1.call-update) | async-done | bytes 16400
  489.7 0.8 copy.30
  490.6 45.1 %all-gather = bf16[2048,64]{1,0:T(8,128)(2,1)S(1)} all-gather(bf16[64,64]{1,0:T(8,128)(2,1)S(1)} %copy.30), channel_id=2, replica_groups=mesh['src'=8,'wch'=8,'wcl'=2,'core'=2] {'src','wcl','core'}, dimensions={0}, use_global_device_ids=true | all-gather | bytes 270336 | tf_op jit(solution)/shard_map/all_gather | solution.py:70
  535.6 1.2 copy.48
  536.8 1.5 reshape.100
  538.3 1.0 fusion.23
  539.3 1.2 fusion.8
  540.5 0.6 copy.49
  (13 shorter events, 0.1 us)
Async XLA Ops:
  7.2 182.4 %copy-start = (bf16[1,6144,256]{2,1,0:T(8,128)(2,1)S(1)}, bf16[1,6144,256]{2,1,0:T(8,128)(2,1)}, u32[]{:S(2)}) copy-start(bf16[1,6144,256]{2,1,0:T(8,128)(2,1)} %param.13) | copy-start | bytes 9437188
  7.2 118.9 %reduce-scatter.6.cloned.1.call-start = ((), (), s32[]{:S(2)}) async-start(), calls=%async_computation.3 | async-start | bytes 6684672 | tf_op jit(solution)/shard_map/reduce_scatter | solution.py:43
  12.0 2.4 copy-start.3
  14.3 3.9 collective-permute-start
  14.4 3.8 collective-permute-start.1
  21.8 167.7 %all-gather.4.cloned.1.call-start = ((), (), s32[]{:S(2)}) async-start(), calls=%async_computation.4 | async-start | bytes 6488064 | tf_op jit(solution)/shard_map/all_gather | solution.py:46
  127.9 153.0 %copy-start.4 = (f32[256]{0:T(256)S(1)}, f32[256]{0:T(256)}, u32[]{:S(2)}) copy-start(f32[256]{0:T(256)} %param.15) | copy-start | bytes 3076
  127.9 151.4 %reduce-scatter.8.cloned.1.call-start = ((), (), s32[]{:S(2)}) async-start(), calls=%async_computation.5 | async-start | bytes 589824 | tf_op jit(solution)/shard_map/reduce_scatter | solution.py:51
  195.0 142.7 %all-gather.6.cloned.1.call-start = ((), (), s32[]{:S(2)}) async-start(), calls=%async_computation.6 | async-start | bytes 2433024 | tf_op jit(solution)/shard_map/all_gather | solution.py:56
  281.5 208.2 %reduce-scatter.10.cloned.1.call-start = ((), (), s32[]{:S(2)}) async-start(), calls=%async_computation.7 | async-start | bytes 1081344
  337.7 1.9 copy-start.1
  337.7 2.3 copy-start.2
  339.9 4.0 copy-start.5
  340.2 3.9 slice-start
Sparse Core Ops, SparseCore 0:
  21.9 104.1 reduce-scatter.5
  128.0 61.5 all-gather.3
  195.1 84.1 reduce-scatter.7
  281.7 55.9 all-gather.5
  344.0 145.6 reduce-scatter.9
